TPU v7x, 512 devices: a whole 4x8x8 slice. The times are simulated.
512 devices in a mesh: pipe: 4 (over z_hi), ctx: 32 (over y, z_lo, core), dp: 4 (over x).
Axes of the slice: x: 4, y: 8, z: 8 (z_hi: 4, z_lo: 2; z = z_hi * 2 + z_lo), core: 2. Of those that a mesh axis runs over, the one named last changes fastest.
Arguments:
- queries: bfloat16 [4, 4, 4096, 4096], P('pipe', 'dp', 'ctx'), may hold values from -7 to 7
- key_input: bfloat16 [4, 4, 4096, 512], P('pipe', 'dp', 'ctx'), may hold values from -4 to 4
- value_input: bfloat16 [4, 4, 4096, 512], P('pipe', 'dp', 'ctx'), may hold values from -6 to 6
- incoming: bfloat16 [4, 4, 4096, 4096], P('pipe', 'dp', 'ctx'), may hold values from -6 to 6
- segments: int32 [4, 4096], P('dp'), may hold values from 0 to 15, never falling along the last dimension, each value on 1 to 512 neighbouring positions
Outputs:
- query_grad: bfloat16 [4, 4, 4096, 4096], P('pipe', 'dp', 'ctx')
- key_grad: bfloat16 [4, 4, 4096, 512], P('pipe', 'dp', 'ctx')
- value_grad: bfloat16 [4, 4, 4096, 512], P('pipe', 'dp', 'ctx')
- bias_grad: float32 [4, 5120], P('pipe')
Inputs may be any that keep to these rules, and one draw needn't show every extreme that they name: `segments`: tokens of one document are contiguous; every document holds 1 to 512 tokens and one holds exactly 512.
All inputs are finite; a program needn't handle non-finite values.
Results may differ from a plain program's by a relative error of at most 0.009.
Values may be sent and summed in bfloat16 or wider, within the bound.
No kernel may reach another device: no remote copies, remote signals or barrier semaphores. Data moves between devices by JAX's collectives and lax.ppermute only.
A program may use at most 64 MiB of HBM per device.

v0:
```python
import math
import jax
import jax.numpy as jnp
from jax import lax
from jax.sharding import PartitionSpec as P

ASKER_STREAMS = 32
SHARED_GROUPS = 4
FEATURE_SIZE = 128
QUERY_PER_KEY = 8


def passed_along(value, axis, steps):
    count = lax.axis_size(axis)
    pairs = [(source, (source + steps) % count) for source in range(count)]
    return lax.ppermute(value, axis, pairs)


def attend(
    queries, key_rows, value_rows, cotangent, query_doc, key_doc, query_pos, key_pos, scaling
):
    scores = (
        jnp.einsum("gqd,kd->gqk", queries, key_rows, preferred_element_type=jnp.float32) * scaling
    )
    visible = (query_doc[:, None] == key_doc[None, :]) & (key_pos[None, :] <= query_pos[:, None])
    scores = jnp.where(visible[None], scores, -1e30)
    row_max = jnp.max(scores, axis=-1, keepdims=True)
    weights = jnp.where(visible[None], jnp.exp(scores - row_max), 0.0)
    probs = weights / jnp.sum(weights, axis=-1, keepdims=True)
    probs_b = probs.astype(jnp.bfloat16)
    attn_out = jnp.einsum("gqk,kd->gqd", probs_b, value_rows, preferred_element_type=jnp.float32)
    dot_out = jnp.sum(cotangent.astype(jnp.float32) * attn_out, axis=-1, keepdims=True)
    grad_prob = jnp.einsum("gqd,kd->gqk", cotangent, value_rows, preferred_element_type=jnp.float32)
    grad_score = (probs * (grad_prob - dot_out) * scaling).astype(jnp.bfloat16)
    asker_derivative = jnp.einsum(
        "gqk,kd->gqd", grad_score, key_rows, preferred_element_type=jnp.float32
    )
    lookup_derivative = jnp.einsum(
        "gqk,gqd->kd", grad_score, queries, preferred_element_type=jnp.float32
    )
    content_derivative = jnp.einsum(
        "gqk,gqd->kd", probs_b, cotangent, preferred_element_type=jnp.float32
    )
    return (asker_derivative, lookup_derivative, content_derivative)


def banded(queries, key_rows, value_rows, cotangent, doc_ids, block_len, scaling):
    length = doc_ids.shape[0]
    blocks = length // block_len
    width = key_rows.shape[1]
    key_pad = jnp.concatenate([jnp.zeros((block_len, width), key_rows.dtype), key_rows], axis=0)
    value_pad = jnp.concatenate(
        [jnp.zeros((block_len, width), value_rows.dtype), value_rows], axis=0
    )
    doc_pad = jnp.concatenate([jnp.full((block_len,), -1, jnp.int32), doc_ids])
    pos_pad = jnp.arange(length + block_len, dtype=jnp.int32) - block_len

    def step(carried, block):
        key_acc, value_acc = carried
        anchor = block * block_len
        query_blk = lax.dynamic_slice_in_dim(queries, anchor, block_len, 1)
        cot_blk = lax.dynamic_slice_in_dim(cotangent, anchor, block_len, 1)
        key_blk = lax.dynamic_slice_in_dim(key_pad, anchor, 2 * block_len, 0)
        value_blk = lax.dynamic_slice_in_dim(value_pad, anchor, 2 * block_len, 0)
        query_doc = lax.dynamic_slice_in_dim(doc_ids, anchor, block_len, 0)
        key_doc = lax.dynamic_slice_in_dim(doc_pad, anchor, 2 * block_len, 0)
        query_pos = anchor + jnp.arange(block_len, dtype=jnp.int32)
        key_pos = lax.dynamic_slice_in_dim(pos_pad, anchor, 2 * block_len, 0)
        asker_derivative, lookup_derivative, content_derivative = attend(
            query_blk, key_blk, value_blk, cot_blk, query_doc, key_doc, query_pos, key_pos, scaling
        )
        key_acc = lax.dynamic_update_slice_in_dim(
            key_acc,
            lax.dynamic_slice_in_dim(key_acc, anchor, 2 * block_len, 0) + lookup_derivative,
            anchor,
            0,
        )
        value_acc = lax.dynamic_update_slice_in_dim(
            value_acc,
            lax.dynamic_slice_in_dim(value_acc, anchor, 2 * block_len, 0) + content_derivative,
            anchor,
            0,
        )
        return ((key_acc, value_acc), asker_derivative)

    start_acc = jnp.zeros((length + block_len, width), jnp.float32)
    (key_acc, value_acc), query_blocks = lax.scan(
        step, (start_acc, start_acc), jnp.arange(blocks, dtype=jnp.int32)
    )
    groups = queries.shape[0]
    asker_derivative = query_blocks.transpose(1, 0, 2, 3).reshape(groups, length, width)
    return (asker_derivative, key_acc[block_len:], value_acc[block_len:])


def body(queries, key_input, value_input, incoming, segments):
    shard_length = queries.shape[2]
    ctx_size = lax.axis_size("ctx")
    reach_dev = min(4, ctx_size - 1)
    block_len = reach_dev * shard_length
    scaling = 1.0 / math.sqrt(FEATURE_SIZE)
    doc_ids = segments[0]
    handed = passed_along(incoming, "pipe", -1)
    query_tok = queries[0, 0].reshape(shard_length, ASKER_STREAMS, FEATURE_SIZE)
    cot_tok = handed[0, 0].reshape(shard_length, ASKER_STREAMS, FEATURE_SIZE)
    key_widened = jnp.repeat(
        key_input[0, 0].reshape(shard_length, SHARED_GROUPS, FEATURE_SIZE), QUERY_PER_KEY, axis=1
    )
    value_widened = jnp.repeat(
        value_input[0, 0].reshape(shard_length, SHARED_GROUPS, FEATURE_SIZE), QUERY_PER_KEY, axis=1
    )
    query_head, key_head, value_head, cot_head = (
        lax.all_to_all(query_tok, "ctx", split_axis=1, concat_axis=0, tiled=True),
        lax.all_to_all(key_widened, "ctx", split_axis=1, concat_axis=0, tiled=True),
        lax.all_to_all(value_widened, "ctx", split_axis=1, concat_axis=0, tiled=True),
        lax.all_to_all(cot_tok, "ctx", split_axis=1, concat_axis=0, tiled=True),
    )

    def per_head(members):
        return banded(
            members[0][None], members[1], members[2], members[3][None], doc_ids, block_len, scaling
        )

    asker_derivative, lookup_derivative, content_derivative = lax.map(
        per_head,
        (
            query_head.transpose(1, 0, 2),
            key_head.transpose(1, 0, 2),
            value_head.transpose(1, 0, 2),
            cot_head.transpose(1, 0, 2),
        ),
    )
    asker_derivative = asker_derivative[:, 0].transpose(1, 0, 2)
    lookup_derivative = lookup_derivative.transpose(1, 0, 2)
    content_derivative = content_derivative.transpose(1, 0, 2)
    query_back, key_backward, value_backward = (
        lax.all_to_all(asker_derivative, "ctx", split_axis=0, concat_axis=1, tiled=True),
        lax.all_to_all(lookup_derivative, "ctx", split_axis=0, concat_axis=1, tiled=True),
        lax.all_to_all(content_derivative, "ctx", split_axis=0, concat_axis=1, tiled=True),
    )
    query_flat = query_back.reshape(shard_length, ASKER_STREAMS * FEATURE_SIZE)
    key_flattened = (
        key_backward.reshape(shard_length, SHARED_GROUPS, QUERY_PER_KEY, FEATURE_SIZE)
        .sum(axis=2)
        .reshape(shard_length, SHARED_GROUPS * FEATURE_SIZE)
    )
    value_flat = (
        value_backward.reshape(shard_length, SHARED_GROUPS, QUERY_PER_KEY, FEATURE_SIZE)
        .sum(axis=2)
        .reshape(shard_length, SHARED_GROUPS * FEATURE_SIZE)
    )
    offset_parts = jnp.concatenate(
        [jnp.sum(query_flat, axis=0), jnp.sum(key_flattened, axis=0), jnp.sum(value_flat, axis=0)]
    )
    offset_overall = lax.psum(offset_parts, ("ctx", "dp"))
    bias_scaled = offset_overall / math.sqrt(lax.axis_size("dp") * shard_length * ctx_size)
    query_grad = query_flat.astype(jnp.bfloat16)[None, None]
    key_grad = key_flattened.astype(jnp.bfloat16)[None, None]
    value_grad = value_flat.astype(jnp.bfloat16)[None, None]
    return (query_grad, key_grad, value_grad, bias_scaled[None])


def solution(mesh):
    return jax.shard_map(
        body,
        mesh=mesh,
        in_specs=(
            P("pipe", "dp", "ctx", None),
            P("pipe", "dp", "ctx", None),
            P("pipe", "dp", "ctx", None),
            P("pipe", "dp", "ctx", None),
            P("dp", None),
        ),
        out_specs=(
            P("pipe", "dp", "ctx", None),
            P("pipe", "dp", "ctx", None),
            P("pipe", "dp", "ctx", None),
            P("pipe", None),
        ),
        check_vma=False,
    )
```

profile of v0, /device:TPU:128, one launch (start us, length us, event | category | flops | bytes accessed | tf_op | source)
XLA Modules:
  0.0 1042.6 jit_solution(12610844461914456718)
XLA Ops:
  2.9 9.3 all-to-all-start.1
  12.2 28.5 %all-to-all-done.1 = bf16[128,32,128]{2,0,1:T(8,128)(2,1)S(1)} async-done(((bf16[128,32,128]{2,0,1:T(8,128)(2,1)}), bf16[128,32,128]{2,0,1:T(8,128)(2,1)S(1)}, u32[]{:S(2)}, u32[]{:S(2)}) %all-to-all-start.1) | async-done | bytes 1048608 | tf_op jit(solution)/shard_map/all_to_all | solution.py:113
  42.0 3.9 all-to-all-start.3
  47.8 37.3 %collective-permute-done = bf16[1,1,128,4096]{3,2,1,0:T(8,128)(2,1)S(1)} collective-permute-done((bf16[1,1,128,4096]{3,2,1,0:T(8,128)(2,1)}, bf16[1,1,128,4096]{3,2,1,0:T(8,128)(2,1)S(1)}, u32[]{:S(2)}, u32[]{:S(2)}) %collective-permute-start) | collective-permute-done | bytes 1048608 | tf_op jit(solution)/shard_map/ppermute | solution.py:16
  86.5 30.7 %all-to-all-start.2 = ((bf16[128,32,128]{0,2,1:T(8,128)(2,1)}), bf16[128,32,128]{0,2,1:T(8,128)(2,1)S(1)}, u32[]{:S(2)}, u32[]{:S(2)}) async-start(bf16[128,32,128]{0,2,1:T(8,128)(2,1)} %bitcast.112), calls=%async_computation.2 | async-start | bytes 2097152 | tf_op jit(solution)/shard_map/all_to_all | solution.py:115
  120.1 25.7 %all-to-all-done.2 = bf16[128,32,128]{0,2,1:T(8,128)(2,1)S(1)} async-done(((bf16[128,32,128]{0,2,1:T(8,128)(2,1)}), bf16[128,32,128]{0,2,1:T(8,128)(2,1)S(1)}, u32[]{:S(2)}, u32[]{:S(2)}) %all-to-all-start.2) | async-done | bytes 1048608 | tf_op jit(solution)/shard_map/all_to_all | solution.py:115
  145.8 4.7 all-to-all-start
  154.3 25.3 %all-to-all-done = bf16[128,32,128]{2,0,1:T(8,128)(2,1)} async-done(((bf16[128,32,128]{2,0,1:T(8,128)(2,1)}), bf16[128,32,128]{2,0,1:T(8,128)(2,1)}, u32[]{:S(2)}, u32[]{:S(2)}) %all-to-all-start) | async-done | bytes 1048608 | tf_op jit(solution)/shard_map/all_to_all | solution.py:112
  183.3 126.4 %while.25 = (s32[]{:T(128)}, f32[4608,128]{1,0:T(8,128)}, f32[4608,128]{1,0:T(8,128)}, f32[8,1,512,128]{3,2,1,0:T(8,128)}, s32[8]{0:T(128)}, /*index=5*/s32[4096...) while((s32[]{:T(128)}, f32[4608,128]{1,0:T(8,128)}, ...), condition=%wide.region_4.5_spmd, body=%wide.region_0.4_spmd.sunk | while | flops 820444160 | bytes 22487844 | solution.py:87
  208.1 2.4 fusion.59
  223.9 2.4 fusion.59
  239.7 2.4 fusion.59
  255.5 2.4 fusion.59
  271.3 2.4 fusion.59
  287.1 2.4 fusion.59
  302.9 2.4 fusion.59
  309.7 3.1 slice.8
  312.8 4.0 all-to-all-start.5
  316.8 3.1 slice.9
  319.9 48.6 %all-to-all-done.5 = f32[4096,1,128]{2,1,0:T(1,128)S(1)} async-done(((f32[4096,1,128]{2,1,0:T(1,128)}), f32[4096,1,128]{2,1,0:T(1,128)S(1)}, u32[]{:S(2)}, u32[]{:S(2)}) %all-to-all-start.5) | async-done | bytes 2097184 | tf_op jit(solution)/shard_map/all_to_all | solution.py:137
  368.5 56.4 %all_to_all.105 = f32[4096,1,128]{2,1,0:T(1,128)} all-to-all(f32[4096,1,128]{2,1,0:T(1,128)} %bitcast.109), channel_id=1, replica_groups=mesh['pipe'=4,'ctx'=32,'dp'=4] {'ctx'}, dimensions={0} | all-to-all | bytes 4194304 | tf_op jit(solution)/shard_map/all_to_all | solution.py:138
  424.9 4.8 all-to-all-start.4
  431.6 49.7 %all-to-all-done.4 = f32[4096,1,128]{2,1,0:T(1,128)} async-done(((f32[4096,1,128]{2,1,0:T(1,128)}), f32[4096,1,128]{2,1,0:T(1,128)}, u32[]{:S(2)}, u32[]{:S(2)}) %all-to-all-start.4) | async-done | bytes 2097184 | tf_op jit(solution)/shard_map/all_to_all | solution.py:136
  484.8 549.9 %psum.7 = f32[5120]{0:T(1024)S(1)} all-reduce(f32[5120]{0:T(1024)S(1)} %pad_maximum_fusion), channel_id=1, replica_groups=mesh['pipe'=4,'ctx'=32,'dp'=4] {'ctx','dp'}, use_global_device_ids=true, to_apply=%region_12.13 | all-reduce | flops 5120 | bytes 40960 | tf_op jit(solution)/shard_map/psum | solution.py:154
  (153 shorter events, 135.0 us)
Async XLA Ops:
  0.6 11.5 %copy-start = (bf16[1,1,128,512]{3,2,1,0:T(8,128)(2,1)S(1)}, bf16[1,1,128,512]{3,2,1,0:T(8,128)(2,1)}, u32[]{:S(2)}) copy-start(bf16[1,1,128,512]{3,2,1,0:T(8,128)(2,1)} %param.9) | copy-start | bytes 393220
  2.9 37.9 %all-to-all-start.1 = ((bf16[128,32,128]{2,0,1:T(8,128)(2,1)}), bf16[128,32,128]{2,0,1:T(8,128)(2,1)S(1)}, u32[]{:S(2)}, u32[]{:S(2)}) async-start(bf16[128,32,128]{2,0,1:T(8,128)(2,1)} %bitcast.9), calls=%async_computation.1 | async-start | bytes 2097152 | tf_op jit(solution)/shard_map/all_to_all | solution.py:113
  42.0 44.5 %all-to-all-start.3 = ((bf16[128,32,128]{2,0,1:T(8,128)(2,1)}), bf16[128,32,128]{2,0,1:T(8,128)(2,1)S(1)}, u32[]{:S(2)}, u32[]{:S(2)}) async-start(bf16[128,32,128]{2,0,1:T(8,128)(2,1)} %bitcast.17), calls=%async_computation.3 | async-start | bytes 2097152 | tf_op jit(solution)/shard_map/all_to_all | solution.py:114
  45.9 39.3 %collective-permute-start = (bf16[1,1,128,4096]{3,2,1,0:T(8,128)(2,1)}, bf16[1,1,128,4096]{3,2,1,0:T(8,128)(2,1)S(1)}, u32[]{:S(2)}, u32[]{:S(2)}) collective-permute-start(bf16[1,1,128,4096]{3,2,1,0:T(8,128)(2,1)} %param.10), channel_id=1, source_target_pairs={{0,384},{128,0},{256,128},{384,256},{1,385},{129,1},{257,129},{385... | collective-permute-start | bytes 3145736 | tf_op jit(solution)/shard_map/ppermute | solution.py:16
  86.5 59.3 %all-to-all-start.2 = ((bf16[128,32,128]{0,2,1:T(8,128)(2,1)}), bf16[128,32,128]{0,2,1:T(8,128)(2,1)S(1)}, u32[]{:S(2)}, u32[]{:S(2)}) async-start(bf16[128,32,128]{0,2,1:T(8,128)(2,1)} %bitcast.112), calls=%async_computation.2 | async-start | bytes 2097152 | tf_op jit(solution)/shard_map/all_to_all | solution.py:115
  118.7 31.8 %copy-start.1 = (s32[1,4096]{1,0:T(1,128)S(1)}, s32[1,4096]{1,0:T(1,128)}, u32[]{:S(2)}) copy-start(s32[1,4096]{1,0:T(1,128)} %param.11) | copy-start | bytes 49156
  145.8 33.8 %all-to-all-start = ((bf16[128,32,128]{2,0,1:T(8,128)(2,1)}), bf16[128,32,128]{2,0,1:T(8,128)(2,1)}, u32[]{:S(2)}, u32[]{:S(2)}) async-start(bf16[128,32,128]{2,0,1:T(8,128)(2,1)} %copy.41), calls=%async_computation | async-start | bytes 2097152 | tf_op jit(solution)/shard_map/all_to_all | solution.py:112
  312.8 55.7 %all-to-all-start.5 = ((f32[4096,1,128]{2,1,0:T(1,128)}), f32[4096,1,128]{2,1,0:T(1,128)S(1)}, u32[]{:S(2)}, u32[]{:S(2)}) async-start(f32[4096,1,128]{2,1,0:T(1,128)} %bitcast.108), calls=%async_computation.5 | async-start | bytes 4194304 | tf_op jit(solution)/shard_map/all_to_all | solution.py:137
  424.9 56.4 %all-to-all-start.4 = ((f32[4096,1,128]{2,1,0:T(1,128)}), f32[4096,1,128]{2,1,0:T(1,128)}, u32[]{:S(2)}, u32[]{:S(2)}) async-start(f32[4096,1,128]{2,1,0:T(1,128)} %bitcast.116), calls=%async_computation.4 | async-start | bytes 4194304 | tf_op jit(solution)/shard_map/all_to_all | solution.py:136
where the time goes:
time: 1050 us; the launch traced here: 1040 us
  blocking collectives  606 us (58%)
  waiting for transfers between devices  215 us (20%)
  matrix products  76.1 us (7%)
  starting transfers between devices  59.3 us (6%)
  local copies, waits for them, and re-layouts  57 us (5%)
  other arithmetic  23 us (2%)
    psum x1, blocking collectives, body(): offset_overall = lax.psum(offset_parts, ('ctx', 'dp'))  550 us
    all_to_all x1, blocking collectives, body(): lax.all_to_all(content_derivative, 'ctx', split_axis=0, concat_axis=1, ti...  56.4 us
    all_to_all x1, waiting for transfers between devices, body(): lax.all_to_all(asker_derivative, 'ctx', split_axis=0, concat_axis=1, tile...  49.7 us
    all_to_all x1, waiting for transfers between devices, body(): lax.all_to_all(lookup_derivative, 'ctx', split_axis=0, concat_axis=1, til...  48.6 us
    ppermute x1, waiting for transfers between devices, passed_along(): return lax.ppermute(value, axis, pairs)  37.3 us
    all_to_all x1, starting transfers between devices, body(): lax.all_to_all(cot_tok, 'ctx', split_axis=1, concat_axis=0, tiled=True)  30.7 us
    all_to_all x1, waiting for transfers between devices, body(): lax.all_to_all(key_widened, 'ctx', split_axis=1, concat_axis=0, tiled=True)  28.5 us
    all_to_all x1, waiting for transfers between devices, body(): lax.all_to_all(cot_tok, 'ctx', split_axis=1, concat_axis=0, tiled=True)  25.7 us
  transfers between devices with their start and end apart: 7, of which 6 were waited for; matrix products, arithmetic and copies ran while one was open for 1% of the time, Pallas kernels for 0%

commit v1 on v0

--- a/solution.py
+++ b/solution.py
@@ -109,7 +109,12 @@
         value_input[0, 0].reshape(shard_length, SHARED_GROUPS, FEATURE_SIZE), QUERY_PER_KEY, axis=1
     )
     query_head, key_head, value_head, cot_head = (
-        lax.all_to_all(query_tok, "ctx", split_axis=1, concat_axis=0, tiled=True),
+        jnp.concatenate(
+            lax.all_to_all(
+                jnp.stack(jnp.split(query_tok, lax.axis_size("ctx"), axis=1)), "ctx", 0, 0
+            ),
+            axis=0,
+        ),
         lax.all_to_all(key_widened, "ctx", split_axis=1, concat_axis=0, tiled=True),
         lax.all_to_all(value_widened, "ctx", split_axis=1, concat_axis=0, tiled=True),
         lax.all_to_all(cot_tok, "ctx", split_axis=1, concat_axis=0, tiled=True),

time: 1050 us -> 1040 us (level)
  the two profiles are of different devices: /device:TPU:128 before, /device:TPU:32 now
where the time goes in v1:
time: 1040 us; the launch traced here: 1030 us
  blocking collectives  613 us (59%)
  waiting for transfers between devices  173 us (17%)
  local copies, waits for them, and re-layouts  79.3 us (8%)
  matrix products  76.1 us (7%)
  starting transfers between devices  63.4 us (6%)
  other arithmetic  23 us (2%)
    psum x1, blocking collectives, body(): offset_overall = lax.psum(offset_parts, ('ctx', 'dp'))  554 us
    all_to_all x1, blocking collectives, body(): lax.all_to_all(content_derivative, 'ctx', split_axis=0, concat_axis=1, ti...  58.2 us
    all_to_all x1, waiting for transfers between devices, body(): lax.all_to_all(asker_derivative, 'ctx', split_axis=0, concat_axis=1, tile...  43.2 us
    all_to_all x1, waiting for transfers between devices, body(): lax.all_to_all(lookup_derivative, 'ctx', split_axis=0, concat_axis=1, til...  42 us
    all_to_all x1, waiting for transfers between devices, body(): lax.all_to_all(key_widened, 'ctx', split_axis=1, concat_axis=0, tiled=True)  36.3 us
    unnamed x41, local copies, waits for them, and re-layouts  23.6 us
  transfers between devices with their start and end apart: 7, of which 6 were waited for; matrix products, arithmetic and copies ran while one was open for 4% of the time, Pallas kernels for 0%

profile of v1, /device:TPU:32, one launch (start us, length us, event | category | flops | bytes accessed | tf_op | source)
XLA Modules:
  0.0 1033.0 jit_solution(4003555196971483441)
XLA Ops:
  0.6 11.1 %collective-permute-start = (bf16[1,1,128,4096]{3,2,1,0:T(8,128)(2,1)}, bf16[1,1,128,4096]{3,2,1,0:T(8,128)(2,1)}, u32[]{:S(2)}, u32[]{:S(2)}) collective-permute-start(bf16[1,1,128,4096]{3,2,1,0:T(8,128)(2,1)} %param.10), channel_id=1, source_target_pairs={{0,384},{128,0},{256,128},{384,256},{1,385},{129,1},{257,129},{385... | collective-permute-start | bytes 3145736 | tf_op jit(solution)/shard_map/ppermute | solution.py:16
  14.0 8.4 all-to-all-start.1
  30.5 36.3 %all-to-all-done.1 = bf16[128,32,128]{2,0,1:T(8,128)(2,1)S(1)} async-done(((bf16[128,32,128]{2,0,1:T(8,128)(2,1)}), bf16[128,32,128]{2,0,1:T(8,128)(2,1)S(1)}, u32[]{:S(2)}, u32[]{:S(2)}) %all-to-all-start.1) | async-done | bytes 1048608 | tf_op jit(solution)/shard_map/all_to_all | solution.py:118
  68.0 7.4 all-to-all-start.3
  83.9 15.7 %all-to-all-done.3 = bf16[128,32,128]{2,0,1:T(8,128)(2,1)S(1)} async-done(((bf16[128,32,128]{2,0,1:T(8,128)(2,1)}), bf16[128,32,128]{2,0,1:T(8,128)(2,1)S(1)}, u32[]{:S(2)}, u32[]{:S(2)}) %all-to-all-start.3) | async-done | bytes 1048608 | tf_op jit(solution)/shard_map/all_to_all | solution.py:119
  99.6 9.0 all-to-all-start.2
  117.0 16.0 %all-to-all-done.2 = bf16[128,32,128]{0,2,1:T(8,128)(2,1)} async-done(((bf16[128,32,128]{0,2,1:T(8,128)(2,1)}), bf16[128,32,128]{0,2,1:T(8,128)(2,1)}, u32[]{:S(2)}, u32[]{:S(2)}) %all-to-all-start.2) | async-done | bytes 1048608 | tf_op jit(solution)/shard_map/all_to_all | solution.py:120
  133.0 9.4 all-to-all-start
  147.2 19.7 %all-to-all-done = bf16[32,128,1,128]{3,1,2,0:T(8,128)(2,1)} async-done(((bf16[32,128,1,128]{3,1,2,0:T(8,128)(2,1)}), bf16[32,128,1,128]{3,1,2,0:T(8,128)(2,1)}, u32[]{:S(2)}, u32[]{:S(2)}) %all-to-all-start) | async-done | bytes 1048608 | tf_op jit(solution)/shard_map/all_to_all | solution.py:113
  170.6 126.8 %while.25 = (s32[]{:T(128)}, f32[4608,128]{1,0:T(8,128)}, f32[4608,128]{1,0:T(8,128)}, f32[8,1,512,128]{3,2,1,0:T(8,128)}, s32[8]{0:T(128)}, /*index=5*/s32[4096...) while((s32[]{:T(128)}, f32[4608,128]{1,0:T(8,128)}, ...), condition=%wide.region_4.5_spmd, body=%wide.region_0.4_spmd.sunk | while | flops 820444160 | bytes 22487844 | solution.py:87
  195.5 2.4 fusion.59
  227.2 2.4 fusion.59
  243.1 2.4 fusion.59
  258.9 2.4 fusion.59
  274.8 2.4 fusion.59
  290.6 2.4 fusion.59
  297.5 3.1 slice.8
  300.6 8.8 all-to-all-start.5
  309.4 3.1 slice.9
  312.4 42.0 %all-to-all-done.5 = f32[4096,1,128]{2,1,0:T(1,128)S(1)} async-done(((f32[4096,1,128]{2,1,0:T(1,128)}), f32[4096,1,128]{2,1,0:T(1,128)S(1)}, u32[]{:S(2)}, u32[]{:S(2)}) %all-to-all-start.5) | async-done | bytes 2097184 | tf_op jit(solution)/shard_map/all_to_all | solution.py:142
  354.4 58.2 %all_to_all.95 = f32[4096,1,128]{2,1,0:T(1,128)} all-to-all(f32[4096,1,128]{2,1,0:T(1,128)} %bitcast.230), channel_id=1, replica_groups=mesh['pipe'=4,'ctx'=32,'dp'=4] {'ctx'}, dimensions={0} | all-to-all | bytes 4194304 | tf_op jit(solution)/shard_map/all_to_all | solution.py:143
  412.7 9.5 all-to-all-start.4
  424.1 43.2 %all-to-all-done.4 = f32[4096,1,128]{2,1,0:T(1,128)} async-done(((f32[4096,1,128]{2,1,0:T(1,128)}), f32[4096,1,128]{2,1,0:T(1,128)}, u32[]{:S(2)}, u32[]{:S(2)}) %all-to-all-start.4) | async-done | bytes 2097184 | tf_op jit(solution)/shard_map/all_to_all | solution.py:141
  470.8 554.4 %psum.7 = f32[5120]{0:T(1024)S(1)} all-reduce(f32[5120]{0:T(1024)S(1)} %pad_maximum_fusion), channel_id=1, replica_groups=mesh['pipe'=4,'ctx'=32,'dp'=4] {'ctx','dp'}, use_global_device_ids=true, to_apply=%region_12.13 | all-reduce | flops 5120 | bytes 40960 | tf_op jit(solution)/shard_map/psum | solution.py:159
  (187 shorter events, 157.8 us)
Async XLA Ops:
  0.6 21.8 %copy-start = (bf16[1,1,128,4096]{3,2,1,0:T(8,128)(2,1)S(1)}, bf16[1,1,128,4096]{3,2,1,0:T(8,128)(2,1)}, u32[]{:S(2)}) copy-start(bf16[1,1,128,4096]{3,2,1,0:T(8,128)(2,1)} %param.7) | copy-start | bytes 3145732
  0.6 80.9 %collective-permute-start = (bf16[1,1,128,4096]{3,2,1,0:T(8,128)(2,1)}, bf16[1,1,128,4096]{3,2,1,0:T(8,128)(2,1)}, u32[]{:S(2)}, u32[]{:S(2)}) collective-permute-start(bf16[1,1,128,4096]{3,2,1,0:T(8,128)(2,1)} %param.10), channel_id=1, source_target_pairs={{0,384},{128,0},{256,128},{384,256},{1,385},{129,1},{257,129},{385... | collective-permute-start | bytes 3145736 | tf_op jit(solution)/shard_map/ppermute | solution.py:16
  14.0 11.0 %copy-start.1 = (bf16[1,1,128,512]{3,2,1,0:T(8,128)(2,1)S(1)}, bf16[1,1,128,512]{3,2,1,0:T(8,128)(2,1)}, u32[]{:S(2)}) copy-start(bf16[1,1,128,512]{3,2,1,0:T(8,128)(2,1)} %param.9) | copy-start | bytes 393220
  14.0 52.8 %all-to-all-start.1 = ((bf16[128,32,128]{2,0,1:T(8,128)(2,1)}), bf16[128,32,128]{2,0,1:T(8,128)(2,1)S(1)}, u32[]{:S(2)}, u32[]{:S(2)}) async-start(bf16[128,32,128]{2,0,1:T(8,128)(2,1)} %bitcast.40), calls=%async_computation.1 | async-start | bytes 2097152 | tf_op jit(solution)/shard_map/all_to_all | solution.py:118
  68.0 31.6 %all-to-all-start.3 = ((bf16[128,32,128]{2,0,1:T(8,128)(2,1)}), bf16[128,32,128]{2,0,1:T(8,128)(2,1)S(1)}, u32[]{:S(2)}, u32[]{:S(2)}) async-start(bf16[128,32,128]{2,0,1:T(8,128)(2,1)} %bitcast.266), calls=%async_computation.3 | async-start | bytes 2097152 | tf_op jit(solution)/shard_map/all_to_all | solution.py:119
  99.6 33.5 %all-to-all-start.2 = ((bf16[128,32,128]{0,2,1:T(8,128)(2,1)}), bf16[128,32,128]{0,2,1:T(8,128)(2,1)}, u32[]{:S(2)}, u32[]{:S(2)}) async-start(bf16[128,32,128]{0,2,1:T(8,128)(2,1)} %bitcast.265), calls=%async_computation.2 | async-start | bytes 2097152 | tf_op jit(solution)/shard_map/all_to_all | solution.py:120
  114.7 27.7 %copy-start.2 = (s32[1,4096]{1,0:T(1,128)S(1)}, s32[1,4096]{1,0:T(1,128)}, u32[]{:S(2)}) copy-start(s32[1,4096]{1,0:T(1,128)} %param.11) | copy-start | bytes 49156
  133.0 33.8 %all-to-all-start = ((bf16[32,128,1,128]{3,1,2,0:T(8,128)(2,1)}), bf16[32,128,1,128]{3,1,2,0:T(8,128)(2,1)}, u32[]{:S(2)}, u32[]{:S(2)}) async-start(bf16[32,128,1,128]{3,1,2,0:T(8,128)(2,1)} %copy.135), calls=%async_computation | async-start | bytes 2097152 | tf_op jit(solution)/shard_map/all_to_all | solution.py:113
  300.6 53.9 %all-to-all-start.5 = ((f32[4096,1,128]{2,1,0:T(1,128)}), f32[4096,1,128]{2,1,0:T(1,128)S(1)}, u32[]{:S(2)}, u32[]{:S(2)}) async-start(f32[4096,1,128]{2,1,0:T(1,128)} %bitcast.229), calls=%async_computation.5 | async-start | bytes 4194304 | tf_op jit(solution)/shard_map/all_to_all | solution.py:142
  412.7 54.6 %all-to-all-start.4 = ((f32[4096,1,128]{2,1,0:T(1,128)}), f32[4096,1,128]{2,1,0:T(1,128)}, u32[]{:S(2)}, u32[]{:S(2)}) async-start(f32[4096,1,128]{2,1,0:T(1,128)} %bitcast.269), calls=%async_computation.4 | async-start | bytes 4194304 | tf_op jit(solution)/shard_map/all_to_all | solution.py:141
